TPU v7x, 32 devices: a whole 2x2x4 slice. The times are simulated.
32 devices in a mesh: dp: 8 (over y, x, core), tensor: 4 (over z).
Axes of the slice: x: 2, y: 2, z: 4, core: 2. Of those that a mesh axis runs over, the one named last changes fastest.
Arguments:
- glu_input: bfloat16 [16, 256, 3072], P('dp', 'tensor'), may hold values from -12 to 12
- depth_kernel: float32 [31, 1536], replicated, may hold values from -1 to 1
- norm_scale: float32 [1536], replicated, may hold values from 0.5 to 1.5
- norm_shift: float32 [1536], replicated, may hold values from -3 to 3
- proj_weight: bfloat16 [1536, 1536], P('tensor'), may hold values from -0.15625 to 0.15625
- out_grad: bfloat16 [16, 256, 1536], P('dp', 'tensor'), may hold values from -6 to 6
Outputs:
- conv_output: bfloat16 [16, 256, 1536], P('dp', 'tensor')
- input_grad: bfloat16 [16, 256, 3072], P('dp', 'tensor')
- weight_grad: float32 [1536, 1536], P('tensor')
- kernel_grad: float32 [31, 1536], replicated
- scale_grad: float32 [1536], replicated
- shift_grad: float32 [1536], replicated
All inputs are finite; a program needn't handle non-finite values.
Results may differ from a plain program's by a relative error of at most 0.0057.
Values may be sent and summed in bfloat16 or wider, within the bound.
No kernel may reach another device: no remote copies, remote signals or barrier semaphores. Data moves between devices by JAX's collectives and lax.ppermute only.
A program may use at most 128 MiB of HBM per device.

v0:
```python
import jax
import jax.numpy as jnp
from jax import lax
from jax.sharding import PartitionSpec as P

epsilon = 1e-05


def extended(array, sides, width):
    for axis, dim in sides:
        peers, length = (lax.axis_size(axis), array.shape[dim])
        up = [(i, (i + 1) % peers) for i in range(peers - 1)]
        down = [(j, i) for i, j in up]
        last = lax.slice_in_dim(array, length - width, length, axis=dim)
        leading = lax.slice_in_dim(array, 0, width, axis=dim)
        before = lax.ppermute(last, axis, up)
        after = lax.ppermute(leading, axis, down)
        array = jnp.concatenate([before, array, after], axis=dim)
    return array


def on_device(glu_input, depth_kernel, norm_scale, norm_shift, proj_weight, out_grad):
    width = proj_weight.shape[1]
    frames = glu_input.shape[1]
    taps = depth_kernel.shape[0]
    radius = (taps - 1) // 2
    everyone = glu_input.shape[0] * frames * lax.axis_size("dp") * lax.axis_size("tensor")
    values = glu_input[..., :width].astype(jnp.float32)
    gates = jax.nn.sigmoid(glu_input[..., width:].astype(jnp.float32))
    gated = (values * gates).astype(jnp.bfloat16)
    padded = extended(gated, (("tensor", 1),), radius)
    conv_out = jnp.zeros(gated.shape, jnp.float32)
    for offset in range(taps):
        conv_out = conv_out + depth_kernel[offset] * padded[:, offset : offset + frames, :]
    average = lax.psum(jnp.sum(conv_out, axis=(0, 1)), ("dp", "tensor")) / everyone
    centred = conv_out - average
    variance = lax.psum(jnp.sum(centred * centred, axis=(0, 1)), ("dp", "tensor")) / everyone
    inverse = lax.rsqrt(variance + epsilon)
    normed = centred * inverse
    affine = norm_scale * normed + norm_shift
    sig_affine = jax.nn.sigmoid(affine)
    activated = (affine * sig_affine).astype(jnp.bfloat16)
    full_weight = lax.all_gather(proj_weight, "tensor", axis=0, tiled=True)
    conv_output = jnp.einsum(
        "btc,cd->btd", activated, full_weight, preferred_element_type=jnp.float32
    ).astype(jnp.bfloat16)
    grad_act = jnp.einsum("btd,cd->btc", out_grad, full_weight, preferred_element_type=jnp.float32)
    grad_affine = grad_act * (sig_affine + affine * sig_affine * (1.0 - sig_affine))
    shift_grad, scale_grad = lax.psum(
        (jnp.sum(grad_affine, axis=(0, 1)), jnp.sum(grad_affine * normed, axis=(0, 1))),
        ("dp", "tensor"),
    )
    grad_conv = (
        norm_scale
        * inverse
        * (grad_affine - shift_grad / everyone - normed * scale_grad / everyone)
    ).astype(jnp.bfloat16)
    grad_pad = extended(grad_conv, (("tensor", 1),), radius)
    grad_gated = jnp.zeros(gated.shape, jnp.float32)
    for offset in range(taps):
        begin = 2 * radius - offset
        grad_gated = grad_gated + depth_kernel[offset] * grad_pad[:, begin : begin + frames, :]
    grad_wide = grad_conv.astype(jnp.float32)
    kernel_terms = jnp.stack(
        [
            jnp.sum(
                padded[:, offset : offset + frames, :].astype(jnp.float32) * grad_wide, axis=(0, 1)
            )
            for offset in range(taps)
        ]
    )
    kernel_grad = lax.psum(kernel_terms, ("dp", "tensor"))
    input_grad = jnp.concatenate(
        [grad_gated * gates, grad_gated * values * gates * (1.0 - gates)], axis=-1
    ).astype(jnp.bfloat16)
    partial_sum = jnp.einsum("btc,btd->cd", activated, out_grad, preferred_element_type=jnp.float32)
    received = lax.all_to_all(partial_sum[None], "tensor", split_axis=1, concat_axis=0, tiled=True)
    local_grad = jnp.sum(received, axis=0)
    weight_grad = lax.psum(local_grad, "dp")
    return (conv_output, input_grad, weight_grad, kernel_grad, scale_grad, shift_grad)


def solution(mesh):
    in_specs = (P("dp", "tensor", None), P(), P(), P(), P("tensor", None), P("dp", "tensor", None))
    out_specs = (P("dp", "tensor", None), P("dp", "tensor", None), P("tensor", None), P(), P(), P())
    return jax.shard_map(
        on_device, mesh=mesh, in_specs=in_specs, out_specs=out_specs, check_vma=False
    )
```

profile of v0, /device:TPU:0, one launch (start us, length us, event | category | flops | bytes accessed | tf_op | source)
XLA Modules:
  0.0 659.3 jit_solution(2058861156043940140)
XLA Ops:
  7.2 1.4 fusion.10
  8.6 4.9 collective-permute-start
  13.5 1.3 collective-permute-start.1
  14.8 1.8 slice_reduce_fusion.30
  16.6 1.4 slice_reduce_fusion.29
  18.0 2.0 collective-permute-done.1
  20.0 3.8 fusion.154
  23.9 40.6 %psum.42 = f32[1536]{0:T(1024)S(1)} all-reduce(f32[1536]{0:T(1024)S(1)} %get-tuple-element.75), channel_id=1, replica_groups=mesh['dp'=8,'tensor'=4] {'dp','tensor'}, use_global_device_ids=true, to_apply=%region_1.0 | all-reduce | flops 1536 | bytes 12288 | tf_op jit(solution)/shard_map/psum | solution.py:35
  64.6 39.4 %psum.43 = f32[1536]{0:T(1024)S(1)} all-reduce(f32[1536]{0:T(1024)S(1)} %multiply_reduce_fusion.1), channel_id=1, replica_groups=mesh['dp'=8,'tensor'=4] {'dp','tensor'}, use_global_device_ids=true, to_apply=%region_3.0 | all-reduce | flops 1536 | bytes 12288 | tf_op jit(solution)/shard_map/psum | solution.py:37
  104.0 0.7 fusion.149
  104.7 2.2 convolution_bitcast_fusion
  106.8 35.9 %copy.12 = f32[1,1536,1536]{2,0,1:T(1,128)} copy(f32[1,1536,1536]{2,1,0:T(8,128)S(1)} %convolution_bitcast_fusion) | data formatting | bytes 18874368 | tf_op jit(solution)/shard_map/broadcast_in_dim | solution.py:77
  142.8 5.9 all-to-all-start
  148.8 0.7 all-gather.2.cloned.1.call-update
  149.5 167.6 %all-gather.2.cloned.1.call-done = bf16[1536,1536]{1,0:T(8,128)(2,1)} async-done(((bf16[384,1536]{1,0:T(8,128)(2,1)}), bf16[1536,1536]{1,0:T(8,128)(2,1)}) %all-gather.2.cloned.1.call-update) | async-done | bytes 4718608 | tf_op jit(solution)/shard_map/all_gather | solution.py:43
  317.1 4.1 fusion.152
  321.2 128.5 %all-reduce = (f32[1536]{0:T(1024)S(1)}, f32[1536]{0:T(1024)S(1)}) all-reduce(f32[1536]{0:T(1024)S(1)} %get-tuple-element.38, f32[1536]{0:T(1024)S(1)} %get-tuple-element.37), channel_id=1, replica_groups=mesh['dp'=8,'tensor'=4] {'dp','tensor'}, use_global_device_ids=true, to_apply=%region_7.0 | all-reduce | flops 3072 | bytes 24576 | tf_op jit(solution)/shard_map/psum | solution.py:49
  449.7 1.5 fusion.90
  451.3 0.9 fusion.89
  452.4 1.2 fusion.74
  453.6 0.8 fusion.73
  454.6 2.8 stack.127
  457.4 1.3 collective-permute-start.2
  458.7 4.6 collective-permute-start.3
  463.3 4.0 fusion.7
  467.3 8.2 %copy.13 = f32[1,1536,1536]{2,1,0:T(8,128)} copy(f32[1,1536,1536]{2,0,1:T(1,128)} %all-to-all-done) | data formatting | bytes 18874368
  475.5 6.5 reduce_sum.328
  482.0 4.1 multiply_convert_fusion
  486.4 1.0 pad_maximum_fusion
  487.4 93.8 %all-reduce.6.cloned.1.call-done = f32[31,1536]{1,0:T(8,128)} async-done(((f32[31,1536]{1,0:T(8,128)}), f32[31,1536]{1,0:T(8,128)}) %all-reduce.6.cloned.1.call-update) | async-done | bytes 190480 | tf_op jit(solution)/shard_map/psum | solution.py:72
  581.2 67.7 %all-reduce.4.cloned.1.call-done = f32[384,1536]{1,0:T(8,128)} async-done(((f32[384,1536]{1,0:T(8,128)}), f32[384,1536]{1,0:T(8,128)}) %all-reduce.4.cloned.1.call-update) | async-done | bytes 2359312 | tf_op jit(solution)/shard_map/psum | solution.py:79
  648.9 3.2 copy.16
  (61 shorter events, 1.5 us)
Async XLA Ops:
  7.2 97.5 %copy-start = (bf16[2,64,1536]{2,1,0:T(8,128)(2,1)S(1)}, bf16[2,64,1536]{2,1,0:T(8,128)(2,1)}, u32[]{:S(2)}) copy-start(bf16[2,64,1536]{2,1,0:T(8,128)(2,1)} %param.11) | copy-start | bytes 1179652
  8.6 9.4 %collective-permute-start = (bf16[2,15,1536]{2,1,0:T(8,128)(2,1)S(1)}, bf16[2,15,1536]{2,1,0:T(8,128)(2,1)S(1)}, u32[]{:S(2)}, u32[]{:S(2)}) collective-permute-start(bf16[2,15,1536]{2,1,0:T(8,128)(2,1)S(1)} %get-tuple-element.79), channel_id=1, source_target_pairs={{0,1},{1,2},{2,3},{4,5},{5,6},{6,7},{8,9},{9,10},{10,11},{12,13},{... | collective-permute-start | bytes 276488 | tf_op jit(solution)/shard_map/ppermute | solution.py:16
  13.5 6.5 collective-permute-start.1
  142.8 174.4 %copy-start.3 = (f32[1536]{0:T(1024)S(1)}, f32[1536]{0:T(1024)}, u32[]{:S(2)}) copy-start(f32[1536]{0:T(1024)} %param.8) | copy-start | bytes 18436
  142.8 174.4 %copy-start.4 = (f32[1536]{0:T(1024)S(1)}, f32[1536]{0:T(1024)}, u32[]{:S(2)}) copy-start(f32[1536]{0:T(1024)} %param.9) | copy-start | bytes 18436
  142.8 324.5 %all-to-all-start = ((f32[1,1536,1536]{2,0,1:T(1,128)}), f32[1,1536,1536]{2,0,1:T(1,128)}, u32[]{:S(2)}, u32[]{:S(2)}) async-start(f32[1,1536,1536]{2,0,1:T(1,128)} %copy.12), calls=%async_computation | async-start | bytes 18874368 | tf_op jit(solution)/shard_map/all_to_all | solution.py:77
  148.7 168.4 %all-gather.2.cloned.1.call-start = ((), (), s32[]{:S(2)}) async-start(), calls=%async_computation.1 | async-start | bytes 5898240 | tf_op jit(solution)/shard_map/all_gather | solution.py:43
  149.4 431.7 %all-reduce.6.cloned.1.call-start = ((), (), s32[]{:S(2)}) async-start(), calls=%async_computation.3 | async-start | bytes 393216 | tf_op jit(solution)/shard_map/psum | solution.py:72
  449.7 17.6 %copy-start.5 = (f32[1536]{0:T(1024)}, f32[1536]{0:T(1024)S(1)}, u32[]{:S(2)}) copy-start(f32[1536]{0:T(1024)S(1)} %get-tuple-element.88) | copy-start | bytes 18436
  449.7 17.6 %copy-start.6 = (f32[1536]{0:T(1024)}, f32[1536]{0:T(1024)S(1)}, u32[]{:S(2)}) copy-start(f32[1536]{0:T(1024)S(1)} %get-tuple-element.89) | copy-start | bytes 18436
  457.3 191.6 %all-reduce.4.cloned.1.call-start = ((), (), s32[]{:S(2)}) async-start(), calls=%async_computation.2 | async-start | bytes 4718592 | tf_op jit(solution)/shard_map/psum | solution.py:79
  457.4 24.6 %collective-permute-start.2 = (bf16[2,15,1536]{2,1,0:T(8,128)(2,1)S(1)}, bf16[2,15,1536]{2,1,0:T(8,128)(2,1)S(1)}, u32[]{:S(2)}, u32[]{:S(2)}) collective-permute-start(bf16[2,15,1536]{2,1,0:T(8,128)(2,1)S(1)} %get-tuple-element.77), channel_id=1, source_target_pairs={{1,0},{2,1},{3,2},{5,4},{6,5},{7,6},{9,8},{10,9},{11,10},{13,12},{... | collective-permute-start | bytes 276488 | tf_op jit(solution)/shard_map/ppermute | solution.py:17
  458.7 23.3 %collective-permute-start.3 = (bf16[2,15,1536]{2,1,0:T(8,128)(2,1)S(1)}, bf16[2,15,1536]{2,1,0:T(8,128)(2,1)S(1)}, u32[]{:S(2)}, u32[]{:S(2)}) collective-permute-start(bf16[2,15,1536]{2,1,0:T(8,128)(2,1)S(1)} %get-tuple-element.78), channel_id=1, source_target_pairs={{0,1},{1,2},{2,3},{4,5},{5,6},{6,7},{8,9},{9,10},{10,11},{12,13},{... | collective-permute-start | bytes 276488 | tf_op jit(solution)/shard_map/ppermute | solution.py:16
  475.5 6.5 copy-start.1
  581.2 70.9 %copy-start.2 = (f32[31,1536]{1,0:T(8,128)S(1)}, f32[31,1536]{1,0:T(8,128)}, u32[]{:S(2)}) copy-start(f32[31,1536]{1,0:T(8,128)} %all-reduce.6.cloned.1.call-done) | copy-start | bytes 571396
Sparse Core Ops, SparseCore 0:
  151.1 165.9 all-gather.1
  457.5 123.6 all-reduce.5
  585.0 63.8 all-reduce.3
where the time goes:
time: 660 us; the launch traced here: 659 us
  waiting for transfers between devices  332 us (50%)
  blocking collectives  208 us (32%)
  local copies, waits for them, and re-layouts  54.2 us (8%)
  other arithmetic  22.2 us (3%)
  starting transfers between devices  18.1 us (3%)
  between operations  14.2 us (2%)
  matrix products  10.2 us (2%)
    all_gather x1, waiting for transfers between devices, on_device(): full_weight = lax.all_gather(proj_weight, 'tensor', axis=0, tiled=True)  168 us
    psum x1, blocking collectives, on_device(): lax.psum((jnp.sum(grad_affine, axis=(0, 1)), jnp.sum(grad_affine * normed...  129 us
    psum x1, waiting for transfers between devices, on_device(): kernel_grad = lax.psum(kernel_terms, ('dp', 'tensor'))  93.8 us
    psum x1, waiting for transfers between devices, on_device(): weight_grad = lax.psum(local_grad, 'dp')  67.7 us
    psum x1, blocking collectives, on_device(): lax.psum(jnp.sum(conv_out, axis=(0, 1)), ('dp', 'tensor')) / everyone  40.6 us
    psum x1, blocking collectives, on_device(): lax.psum(jnp.sum(centred * centred, axis=(0, 1)), ('dp', 'tensor'))  39.4 us
    broadcast_in_dim x1, local copies, waits for them, and re-layouts, on_device(): partial_sum[None]  35.9 us
  transfers between devices with their start and end apart: 8, of which 4 were waited for; matrix products, arithmetic and copies ran while one was open for 6% of the time, Pallas kernels for 0%

commit v1 on v0

--- a/solution.py
+++ b/solution.py
@@ -34,7 +34,10 @@
         conv_out = conv_out + depth_kernel[offset] * padded[:, offset : offset + frames, :]
     average = lax.psum(jnp.sum(conv_out, axis=(0, 1)), ("dp", "tensor")) / everyone
     centred = conv_out - average
-    variance = lax.psum(jnp.sum(centred * centred, axis=(0, 1)), ("dp", "tensor")) / everyone
+    variance = (
+        jnp.sum(lax.all_gather(jnp.sum(centred * centred, axis=(0, 1)), ("dp", "tensor")), axis=0)
+        / everyone
+    )
     inverse = lax.rsqrt(variance + epsilon)
     normed = centred * inverse
     affine = norm_scale * normed + norm_shift

time: 660 us -> 682 us (1.033)
  blocking collectives: 208 us -> 236 us
    all_gather x0 -> x1, blocking collectives: none -> 67.5 us  [on_device(): lax.all_gather(jnp.sum(centred * centred, axis=(0, 1)), ('dp', 'tensor'))]
    psum x1 -> x0, blocking collectives: 39.4 us -> none  [on_device(): lax.psum(jnp.sum(centred * centred, axis=(0, 1)), ('dp', 'tensor'))]
where the time goes in v1:
time: 682 us; the launch traced here: 681 us
  waiting for transfers between devices  328 us (48%)
  blocking collectives  236 us (35%)
  local copies, waits for them, and re-layouts  54.3 us (8%)
  other arithmetic  21.6 us (3%)
  starting transfers between devices  18 us (3%)
  between operations  14.2 us (2%)
  matrix products  9.46 us (1%)
    all_gather x1, waiting for transfers between devices, on_device(): full_weight = lax.all_gather(proj_weight, 'tensor', axis=0, tiled=True)  164 us
    psum x1, blocking collectives, on_device(): lax.psum((jnp.sum(grad_affine, axis=(0, 1)), jnp.sum(grad_affine * normed...  128 us
    psum x1, waiting for transfers between devices, on_device(): kernel_grad = lax.psum(kernel_terms, ('dp', 'tensor'))  93 us
    psum x1, waiting for transfers between devices, on_device(): weight_grad = lax.psum(local_grad, 'dp')  67.7 us
    all_gather x1, blocking collectives, on_device(): lax.all_gather(jnp.sum(centred * centred, axis=(0, 1)), ('dp', 'tensor'))  67.5 us
    psum x1, blocking collectives, on_device(): lax.psum(jnp.sum(conv_out, axis=(0, 1)), ('dp', 'tensor')) / everyone  40.6 us
    broadcast_in_dim x1, local copies, waits for them, and re-layouts, on_device(): partial_sum[None]  35.9 us
  transfers between devices with their start and end apart: 8, of which 4 were waited for; matrix products, arithmetic and copies ran while one was open for 6% of the time, Pallas kernels for 0%

profile of v1, /device:TPU:0, one launch (start us, length us, event | category | flops | bytes accessed | tf_op | source)
XLA Modules:
  0.0 680.8 jit_solution(1181066866923348793)
XLA Ops:
  7.2 1.4 fusion.10
  8.6 4.9 collective-permute-start
  13.6 1.3 collective-permute-start.1
  14.9 1.8 slice_reduce_fusion.30
  16.6 1.4 slice_reduce_fusion.29
  18.1 2.0 collective-permute-done.1
  20.1 3.8 fusion.154
  23.9 40.6 %psum.35 = f32[1536]{0:T(1024)S(1)} all-reduce(f32[1536]{0:T(1024)S(1)} %get-tuple-element.75), channel_id=1, replica_groups=mesh['dp'=8,'tensor'=4] {'dp','tensor'}, use_global_device_ids=true, to_apply=%region_1.0 | all-reduce | flops 1536 | bytes 12288 | tf_op jit(solution)/shard_map/psum | solution.py:35
  64.6 67.5 %all-gather.1 = f32[32,1,1536]{2,1,0:T(1,128)S(1)} all-gather(f32[1,1,1536]{2,1,0:T(1,128)S(1)} %reshape.58), channel_id=2, replica_groups=mesh['dp'=8,'tensor'=4] {'dp','tensor'}, dimensions={0}, use_global_device_ids=true | all-gather | bytes 202752 | tf_op jit(solution)/shard_map/all_gather | solution.py:38
  132.2 1.5 convolution_bitcast_fusion
  133.7 35.9 %copy.12 = f32[1,1536,1536]{2,0,1:T(1,128)} copy(f32[1,1536,1536]{2,1,0:T(8,128)S(1)} %convolution_bitcast_fusion) | data formatting | bytes 18874368 | tf_op jit(solution)/shard_map/broadcast_in_dim | solution.py:80
  169.6 5.8 all-to-all-start
  175.5 0.7 all-gather.4.cloned.1.call-update
  176.2 164.1 %all-gather.4.cloned.1.call-done = bf16[1536,1536]{1,0:T(8,128)(2,1)} async-done(((bf16[384,1536]{1,0:T(8,128)(2,1)}), bf16[1536,1536]{1,0:T(8,128)(2,1)}) %all-gather.4.cloned.1.call-update) | async-done | bytes 4718608 | tf_op jit(solution)/shard_map/all_gather | solution.py:46
  340.3 4.1 fusion.152
  344.4 127.7 %all-reduce = (f32[1536]{0:T(1024)S(1)}, f32[1536]{0:T(1024)S(1)}) all-reduce(f32[1536]{0:T(1024)S(1)} %get-tuple-element.38, f32[1536]{0:T(1024)S(1)} %get-tuple-element.37), channel_id=1, replica_groups=mesh['dp'=8,'tensor'=4] {'dp','tensor'}, use_global_device_ids=true, to_apply=%region_7.0 | all-reduce | flops 3072 | bytes 24576 | tf_op jit(solution)/shard_map/psum | solution.py:52
  472.0 1.5 fusion.90
  473.6 0.9 fusion.89
  474.7 1.2 fusion.74
  475.9 0.8 fusion.73
  476.9 2.8 stack.127
  479.7 1.3 collective-permute-start.2
  481.0 4.6 collective-permute-start.3
  485.6 4.0 fusion.7
  489.6 8.2 %copy.13 = f32[1,1536,1536]{2,1,0:T(8,128)} copy(f32[1,1536,1536]{2,0,1:T(1,128)} %all-to-all-done) | data formatting | bytes 18874368
  497.8 6.5 reduce_sum.338
  504.3 4.1 multiply_convert_fusion
  508.7 1.0 pad_maximum_fusion
  509.7 93.0 %all-reduce.6.cloned.1.call-done = f32[31,1536]{1,0:T(8,128)} async-done(((f32[31,1536]{1,0:T(8,128)}), f32[31,1536]{1,0:T(8,128)}) %all-reduce.6.cloned.1.call-update) | async-done | bytes 190480 | tf_op jit(solution)/shard_map/psum | solution.py:75
  602.6 67.7 %all-reduce.4.cloned.1.call-done = f32[384,1536]{1,0:T(8,128)} async-done(((f32[384,1536]{1,0:T(8,128)}), f32[384,1536]{1,0:T(8,128)}) %all-reduce.4.cloned.1.call-update) | async-done | bytes 2359312 | tf_op jit(solution)/shard_map/psum | solution.py:82
  670.3 3.2 copy.16
  673.6 0.7 copy.17
  (63 shorter events, 1.0 us)
Async XLA Ops:
  7.2 125.1 %copy-start = (bf16[2,64,1536]{2,1,0:T(8,128)(2,1)S(1)}, bf16[2,64,1536]{2,1,0:T(8,128)(2,1)}, u32[]{:S(2)}) copy-start(bf16[2,64,1536]{2,1,0:T(8,128)(2,1)} %param.11) | copy-start | bytes 1179652
  7.2 125.0 %copy-start.3 = (f32[1536]{0:T(1024)S(1)}, f32[1536]{0:T(1024)}, u32[]{:S(2)}) copy-start(f32[1536]{0:T(1024)} %param.8) | copy-start | bytes 18436
  7.2 125.0 %copy-start.4 = (f32[1536]{0:T(1024)S(1)}, f32[1536]{0:T(1024)}, u32[]{:S(2)}) copy-start(f32[1536]{0:T(1024)} %param.9) | copy-start | bytes 18436
  8.6 9.4 %collective-permute-start = (bf16[2,15,1536]{2,1,0:T(8,128)(2,1)S(1)}, bf16[2,15,1536]{2,1,0:T(8,128)(2,1)S(1)}, u32[]{:S(2)}, u32[]{:S(2)}) collective-permute-start(bf16[2,15,1536]{2,1,0:T(8,128)(2,1)S(1)} %get-tuple-element.79), channel_id=1, source_target_pairs={{0,1},{1,2},{2,3},{4,5},{5,6},{6,7},{8,9},{9,10},{10,11},{12,13},{... | collective-permute-start | bytes 276488 | tf_op jit(solution)/shard_map/ppermute | solution.py:16
  13.6 6.5 collective-permute-start.1
  169.6 320.0 %all-to-all-start = ((f32[1,1536,1536]{2,0,1:T(1,128)}), f32[1,1536,1536]{2,0,1:T(1,128)}, u32[]{:S(2)}, u32[]{:S(2)}) async-start(f32[1,1536,1536]{2,0,1:T(1,128)} %copy.12), calls=%async_computation | async-start | bytes 18874368 | tf_op jit(solution)/shard_map/all_to_all | solution.py:80
  175.4 164.9 %all-gather.4.cloned.1.call-start = ((), (), s32[]{:S(2)}) async-start(), calls=%async_computation.1 | async-start | bytes 5898240 | tf_op jit(solution)/shard_map/all_gather | solution.py:46
  176.2 426.5 %all-reduce.6.cloned.1.call-start = ((), (), s32[]{:S(2)}) async-start(), calls=%async_computation.3 | async-start | bytes 393216 | tf_op jit(solution)/shard_map/psum | solution.py:75
  472.0 17.5 %copy-start.5 = (f32[1536]{0:T(1024)}, f32[1536]{0:T(1024)S(1)}, u32[]{:S(2)}) copy-start(f32[1536]{0:T(1024)S(1)} %get-tuple-element.88) | copy-start | bytes 18436
  472.0 17.5 %copy-start.6 = (f32[1536]{0:T(1024)}, f32[1536]{0:T(1024)S(1)}, u32[]{:S(2)}) copy-start(f32[1536]{0:T(1024)S(1)} %get-tuple-element.89) | copy-start | bytes 18436
  479.7 190.7 %all-reduce.4.cloned.1.call-start = ((), (), s32[]{:S(2)}) async-start(), calls=%async_computation.2 | async-start | bytes 4718592 | tf_op jit(solution)/shard_map/psum | solution.py:82
  479.7 24.6 %collective-permute-start.2 = (bf16[2,15,1536]{2,1,0:T(8,128)(2,1)S(1)}, bf16[2,15,1536]{2,1,0:T(8,128)(2,1)S(1)}, u32[]{:S(2)}, u32[]{:S(2)}) collective-permute-start(bf16[2,15,1536]{2,1,0:T(8,128)(2,1)S(1)} %get-tuple-element.77), channel_id=1, source_target_pairs={{1,0},{2,1},{3,2},{5,4},{6,5},{7,6},{9,8},{10,9},{11,10},{13,12},{... | collective-permute-start | bytes 276488 | tf_op jit(solution)/shard_map/ppermute | solution.py:17
  481.0 23.3 %collective-permute-start.3 = (bf16[2,15,1536]{2,1,0:T(8,128)(2,1)S(1)}, bf16[2,15,1536]{2,1,0:T(8,128)(2,1)S(1)}, u32[]{:S(2)}, u32[]{:S(2)}) collective-permute-start(bf16[2,15,1536]{2,1,0:T(8,128)(2,1)S(1)} %get-tuple-element.78), channel_id=1, source_target_pairs={{0,1},{1,2},{2,3},{4,5},{5,6},{6,7},{8,9},{9,10},{10,11},{12,13},{... | collective-permute-start | bytes 276488 | tf_op jit(solution)/shard_map/ppermute | solution.py:16
  497.8 6.5 copy-start.1
  602.6 70.9 %copy-start.2 = (f32[31,1536]{1,0:T(8,128)S(1)}, f32[31,1536]{1,0:T(8,128)}, u32[]{:S(2)}) copy-start(f32[31,1536]{1,0:T(8,128)} %all-reduce.6.cloned.1.call-done) | copy-start | bytes 571396
Sparse Core Ops, SparseCore 0:
  177.8 162.4 all-gather.3
  479.8 122.8 all-reduce.5
  606.5 63.8 all-reduce.3
